TPU v7x, 32 devices: a whole 2x2x4 slice. The times are simulated.
32 devices in a mesh: outer: 4 (over z), inner: 8 (over y, x, core).
Axes of the slice: x: 2, y: 2, z: 4, core: 2. Of those that a mesh axis runs over, the one named last changes fastest.
Arguments:
- observations: float32 [2048, 128], P(('outer', 'inner')), may hold values from -18 to 18
- gains: float32 [2048, 128, 128], P(('outer', 'inner')), may hold values from -0.2 to 0.7, as said below
- smoother_gains: float32 [2048, 128, 128], P(('outer', 'inner')), may hold values from -0.2 to 1.05, as said below
- transition: float32 [128, 128], replicated, may hold values from -0.2 to 1.05, as said below
- observation_map: float32 [128, 128], replicated, may hold values from -0.25 to 1.25, as said below
- initial_mean: float32 [128], replicated, may hold values from -12 to 12
Outputs:
- filtered: float32 [2048, 128], P(('outer', 'inner'))
- smoothed: float32 [2048, 128], P(('outer', 'inner'))
Inputs may be any that keep to these rules, and one draw needn't show every extreme that they name: `gains`: each frame's gain is a dense 128 by 128 matrix with entries in this range; nothing else about its structure is promised. `smoother_gains`: each frame's smoother gain is a dense 128 by 128 matrix with entries in this range; nothing else about its structure is promised. `transition`: a dense 128 by 128 matrix. `observation_map`: a dense 128 by 128 matrix.
All inputs are finite; a program needn't handle non-finite values.
Results may differ from a plain program's by a relative error of at most 0.0003.
Values sent between devices are 32-bit elements; how exact they have to be, the bound alone decides.
No kernel may reach another device: no remote copies, remote signals or barrier semaphores. Data moves between devices by JAX's collectives and lax.ppermute only.
A program may use at most 128 MiB of HBM per device.

v0:
```python
import jax
import jax.numpy as jnp
from jax import lax
from jax.sharding import PartitionSpec as P

exact = lax.Precision.HIGHEST
AXES = ("outer", "inner")


def mm(a, b):
    return jnp.matmul(a, b, precision=exact, preferred_element_type=jnp.float32)


def mv(a, v):
    return jnp.einsum("...ij,...j->...i", a, v, precision=exact, preferred_element_type=jnp.float32)


def pair_up(mats, vecs, backward):
    shape = mats.shape
    pm = mats.reshape(shape[:-3] + (shape[-3] // 2, 2) + shape[-2:])
    pv = vecs.reshape(vecs.shape[:-2] + (vecs.shape[-2] // 2, 2, vecs.shape[-1]))
    first, second = (1, 0) if backward else (0, 1)
    m1, m2 = pm[..., first, :, :], pm[..., second, :, :]
    v1, v2 = pv[..., first, :], pv[..., second, :]
    return mm(m2, m1), mv(m2, v1) + v2


def local_tiers(mats, vecs, backward):
    tiers = [(mats, vecs)]
    while tiers[-1][0].shape[0] > 1:
        tiers.append(pair_up(tiers[-1][0], tiers[-1][1], backward))
    return tiers


def spread(tiers, entry, backward):
    width = entry.shape[0]
    states = entry[None, :]
    for height in reversed(range(len(tiers) - 1)):
        mats, vecs = tiers[height]
        half = mats.shape[0] // 2
        pm = mats.reshape(half, 2, width, width)
        pv = vecs.reshape(half, 2, width)
        if backward:
            other = mv(pm[:, 1], states) + pv[:, 1]
            states = jnp.stack((other, states), axis=1)
        else:
            other = mv(pm[:, 0], states) + pv[:, 0]
            states = jnp.stack((states, other), axis=1)
        states = states.reshape(-1, width)
    return mv(tiers[0][0], states) + tiers[0][1]


def pad_pow2(mats, vecs):
    count = mats.shape[-3]
    size = 1
    while size < count:
        size *= 2
    if size > count:
        width = mats.shape[-1]
        eye = jnp.broadcast_to(
            jnp.eye(width, dtype=mats.dtype), mats.shape[:-3] + (size - count, width, width)
        )
        mats = jnp.concatenate((mats, eye), axis=-3)
        zero = jnp.zeros(vecs.shape[:-2] + (size - count, width), vecs.dtype)
        vecs = jnp.concatenate((vecs, zero), axis=-2)
    return mats, vecs


def reduce_maps(mats, vecs, backward):
    mats, vecs = pad_pow2(mats, vecs)
    while mats.shape[-3] > 1:
        mats, vecs = pair_up(mats, vecs, backward)
    return mats[..., 0, :, :], vecs[..., 0, :]


def keep_only(mats, vecs, keep):
    eye = jnp.eye(mats.shape[-1], dtype=jnp.float32)
    mats = jnp.where(keep[:, None, None], mats, eye)
    vecs = jnp.where(keep[:, None], vecs, 0.0)
    return mats, vecs


def pack(mat, vec):
    return jnp.concatenate((mat, vec[None, :]), axis=0)


def group_level(mat, vec, axis, backward):
    gathered = lax.all_gather(pack(mat, vec), axis)
    mats, vecs = gathered[:, :-1], gathered[:, -1]
    me = lax.axis_index(axis)
    index = jnp.arange(mats.shape[0])
    keep = index > me if backward else index < me
    pm, pv = keep_only(mats, vecs, keep)
    both_m = jnp.stack((pm, mats), axis=0)
    both_v = jnp.stack((pv, vecs), axis=0)
    rm, rv = reduce_maps(both_m, both_v, backward)
    return (rm[0], rv[0]), (rm[1], rv[1])


def across(mat, vec, backward):
    (pm, pv), (gm, gv) = group_level(mat, vec, "inner", backward)
    gathered = lax.all_gather(pack(gm, gv), "outer")
    mats, vecs = gathered[:, :-1], gathered[:, -1]
    me = lax.axis_index("outer")
    index = jnp.arange(mats.shape[0])
    keep = index > me if backward else index < me
    om, ov = reduce_maps(*keep_only(mats, vecs, keep), backward)
    return mm(pm, om), mv(pm, ov) + pv


def on_device(observations, gains, smoother_gains, transition, observation_map, initial_mean):
    me = lax.axis_index(AXES)
    devices = lax.axis_size(AXES)
    mapped = mm(observation_map, transition)
    forward_maps = transition[None] - jnp.einsum(
        "tij,jk->tik", gains, mapped, precision=exact, preferred_element_type=jnp.float32
    )
    forward_inputs = mv(gains, observations)
    forward = local_tiers(forward_maps, forward_inputs, False)
    fm, fv = forward[-1][0][0], forward[-1][1][0]
    before_m, before_v = across(fm, fv, False)
    entry_state = mv(before_m, initial_mean) + before_v
    filtered = spread(forward, entry_state, False)

    predicted_all = jnp.dot(
        filtered, transition.T, precision=exact, preferred_element_type=jnp.float32
    )
    offsets = filtered - mv(smoother_gains, predicted_all)
    backward = local_tiers(smoother_gains, offsets, True)
    bm, bv = backward[-1][0][0], backward[-1][1][0]
    last = me == devices - 1
    extra = jnp.where(last, predicted_all[-1], 0.0)
    bv = bv + mv(bm, extra)
    after_m, after_v = across(bm, bv, True)
    after_state = after_v + extra
    smoothed = spread(backward, after_state, True)
    return (filtered, smoothed)


def solution(mesh):
    in_specs = (
        P(AXES, None),
        P(AXES, None, None),
        P(AXES, None, None),
        P(),
        P(),
        P(),
    )
    out_specs = (P(AXES, None), P(AXES, None))
    return jax.shard_map(
        on_device, mesh=mesh, in_specs=in_specs, out_specs=out_specs, check_vma=False
    )
```

profile of v0, /device:TPU:0, one launch (start us, length us, event | category | flops | bytes accessed | tf_op | source)
XLA Modules:
  0.0 155.9 jit_solution(16540724930119882139)
XLA Ops:
  1.5 1.1 convolution_bitcast_fusion.6
  2.6 0.9 copy.280
  3.5 5.7 %bitcast_subtract_fusion = f32[64,128,128]{1,2,0:T(8,128)S(1)} fusion(f32[128,128,1]{0,1,2:T(8,128)S(1)} %convolution_bitcast_fusion.6, f32[64,128,128]{2,1,0:T(8,128)} %param.7, f32[128,128]{0,1:T(8,128)S(1)} %copy.280), kind=kOutput, calls=%fused_computation | convolution fusion | flops 1611661312 | bytes 8519680 | tf_op jit(solution)/shard_map/tij,jk->tik/dot_general | solution.py:115
  9.2 3.7 %fusion.1 = f32[32,128,128]{2,1,0:T(8,128)S(1)} fusion(f32[32,2,128,128]{2,3,1,0:T(8,128)S(1)} %bitcast.780), kind=kOutput, calls=%fused_computation.6 | convolution fusion | flops 805306368 | bytes 6291456 | tf_op jit(solution)/shard_map/dot_general | solution.py:11
  12.9 1.1 fusion.24
  15.5 6.6 %fusion.148 = f32[64,1,128]{2,1,0:T(1,128)S(1)} fusion(f32[64,128,128]{2,1,0:T(8,128)S(1)} %copy-done.5, f32[64,128,1]{1,2,0:T(1,128)S(1)} %bitcast.866), kind=kOutput, calls=%fused_computation.267 | convolution fusion | flops 12582912 | bytes 4259840 | tf_op jit(solution)/shard_map/...ij,...j->...i/dot_general | solution.py:15
  22.0 2.3 %fusion = f32[32,1,128]{2,1,0:T(1,128)S(1)} fusion(f32[32,2,128,128]{2,3,1,0:T(8,128)S(1)} %bitcast.781, f32[32,2,128]{2,1,0:T(2,128)S(1)} %bitcast.823), kind=kOutput, calls=%fused_computation.5 | convolution fusion | flops 6291456 | bytes 2129920 | tf_op jit(solution)/shard_map/...ij,...j->...i/dot_general | solution.py:15
  24.4 1.7 %fusion.23 = f32[16,1,128]{2,1,0:T(1,128)S(1)} fusion(f32[16,2,128,128]{3,2,1,0:T(8,128)S(1)} %bitcast.784, f32[16,2,128]{2,1,0:T(2,128)S(1)} %bitcast.829), kind=kOutput, calls=%fused_computation.53 | convolution fusion | flops 3145728 | bytes 1064960 | tf_op jit(solution)/shard_map/...ij,...j->...i/dot_general | solution.py:15
  30.8 11.4 %all-gather.4 = f32[8,129,128]{2,1,0:T(8,128)S(1)} all-gather(f32[1,129,128]{2,1,0:T(8,128)S(1)} %maximum_bitcast_fusion), channel_id=2, replica_groups=mesh['outer'=4,'inner'=8] {'inner'}, dimensions={0}, use_global_device_ids=true | all-gather | bytes 594432 | tf_op jit(solution)/shard_map/all_gather | solution.py:88
  43.2 1.2 fusion.135
  44.3 0.9 fusion.70
  48.8 14.9 %all-gather.5 = f32[4,129,128]{2,1,0:T(8,128)} all-gather(f32[1,129,128]{2,1,0:T(8,128)S(1)} %maximum_bitcast_fusion.1), channel_id=3, replica_groups=mesh['outer'=4,'inner'=8] {'outer'}, dimensions={0}, use_global_device_ids=true | all-gather | bytes 330240 | tf_op jit(solution)/shard_map/all_gather | solution.py:102
  63.7 1.2 slice_select_fusion.1
  66.5 1.1 fusion.16
  67.8 1.0 fusion.68
  69.7 1.1 fusion.15
  71.8 1.5 fusion.49
  74.9 1.0 add_bitcast_fusion.5
  75.9 1.7 %fusion.25 = f32[16,1,128]{2,1,0:T(1,128)S(1)} fusion(f32[16,128,1]{1,2,0:T(1,128)S(1)} %bitcast.846, f32[16,2,128,128]{3,2,1,0:T(8,128)S(1)} %bitcast.785), kind=kOutput, calls=%fused_computation.55 | convolution fusion | flops 3145728 | bytes 1064960 | tf_op jit(solution)/shard_map/...ij,...j->...i/dot_general | solution.py:15
  78.4 3.5 %fusion.2 = f32[32,1,128]{2,1,0:T(1,128)S(1)} fusion(f32[32,128,1]{1,2,0:T(1,128)S(1)} %bitcast.833, f32[32,2,128,128]{2,3,1,0:T(8,128)} %bitcast.782), kind=kOutput, calls=%fused_computation.7 | convolution fusion | flops 6291456 | bytes 2129920 | tf_op jit(solution)/shard_map/...ij,...j->...i/dot_general | solution.py:15
  81.9 3.6 %fusion.149 = f32[64,1,128]{2,1,0:T(1,128)S(1)} fusion(f32[64,128,128]{1,2,0:T(8,128)S(1)} %copy-done.4, f32[64,128,1]{1,2,0:T(1,128)S(1)} %bitcast.840), kind=kOutput, calls=%fused_computation.268 | convolution fusion | flops 12582912 | bytes 4259840 | tf_op jit(solution)/shard_map/...ij,...j->...i/dot_general | solution.py:15
  85.6 2.2 %fusion.4 = f32[32,128,128]{2,1,0:T(8,128)S(1)} fusion(f32[32,2,128,128]{3,2,1,0:T(8,128)S(1)} %bitcast.777), kind=kOutput, calls=%fused_computation.9 | convolution fusion | flops 805306368 | bytes 6291456 | tf_op jit(solution)/shard_map/dot_general | solution.py:11
  87.9 1.1 fusion.27
  90.8 6.6 %fusion.151 = f32[64,1,128]{2,1,0:T(1,128)S(1)} fusion(f32[64,128,1]{1,2,0:T(1,128)S(1)} %bitcast.828, f32[64,128,128]{2,1,0:T(8,128)S(1)} %copy-done.1), kind=kOutput, calls=%fused_computation.270 | convolution fusion | flops 12582912 | bytes 4259840 | tf_op jit(solution)/shard_map/...ij,...j->...i/dot_general | solution.py:15
  97.4 3.4 %fusion.3 = f32[32,1,128]{2,1,0:T(1,128)S(1)} fusion(f32[32,2,128,128]{3,2,1,0:T(8,128)S(1)} %bitcast.778, f32[32,2,128]{2,1,0:T(2,128)S(1)} %bitcast.826), kind=kOutput, calls=%fused_computation.8 | convolution fusion | flops 6291456 | bytes 2129920 | tf_op jit(solution)/shard_map/...ij,...j->...i/dot_general | solution.py:15
  100.9 1.7 %fusion.28 = f32[16,1,128]{2,1,0:T(1,128)S(1)} fusion(f32[16,2,128,128]{3,2,1,0:T(8,128)S(1)} %bitcast.787, f32[16,2,128]{2,1,0:T(2,128)S(1)} %bitcast.831), kind=kOutput, calls=%fused_computation.58 | convolution fusion | flops 3145728 | bytes 1064960 | tf_op jit(solution)/shard_map/...ij,...j->...i/dot_general | solution.py:15
  109.0 1.0 fusion.12
  110.9 10.2 %all-gather.6 = f32[8,129,128]{2,1,0:T(8,128)S(1)} all-gather(f32[1,129,128]{2,1,0:T(8,128)S(1)} %maximum_bitcast_fusion.2), channel_id=4, replica_groups=mesh['outer'=4,'inner'=8] {'inner'}, dimensions={0}, use_global_device_ids=true | all-gather | bytes 594432 | tf_op jit(solution)/shard_map/all_gather | solution.py:88
  124.5 14.7 %all-gather.7 = f32[4,129,128]{2,1,0:T(8,128)S(1)} all-gather(f32[1,129,128]{2,1,0:T(8,128)S(1)} %maximum_bitcast_fusion.3), channel_id=5, replica_groups=mesh['outer'=4,'inner'=8] {'outer'}, dimensions={0}, use_global_device_ids=true | all-gather | bytes 330240 | tf_op jit(solution)/shard_map/all_gather | solution.py:102
  143.3 1.7 %fusion.26 = f32[16,1,128]{2,1,0:T(1,128)S(1)} fusion(f32[16,128,1]{1,2,0:T(1,128)S(1)} %bitcast.848, f32[16,2,128,128]{3,2,1,0:T(8,128)S(1)} %bitcast.788), kind=kOutput, calls=%fused_computation.56 | convolution fusion | flops 3145728 | bytes 1064960 | tf_op jit(solution)/shard_map/...ij,...j->...i/dot_general | solution.py:15
  145.0 3.4 %fusion.5 = f32[32,1,128]{2,1,0:T(1,128)S(1)} fusion(f32[32,128,1]{1,2,0:T(1,128)S(1)} %bitcast.835, f32[32,2,128,128]{3,2,1,0:T(8,128)S(1)} %bitcast.779), kind=kOutput, calls=%fused_computation.10 | convolution fusion | flops 6291456 | bytes 2129920 | tf_op jit(solution)/shard_map/...ij,...j->...i/dot_general | solution.py:15
  148.5 6.6 %fusion.152 = f32[64,1,128]{2,1,0:T(1,128)S(1)} fusion(f32[64,128,1]{1,2,0:T(1,128)S(1)} %bitcast.841, f32[64,128,128]{2,1,0:T(8,128)S(1)} %copy-done.2), kind=kOutput, calls=%fused_computation.271 | convolution fusion | flops 12582912 | bytes 4259840 | tf_op jit(solution)/shard_map/...ij,...j->...i/dot_general | solution.py:15
  (200 shorter events, 34.5 us)
Async XLA Ops:
  0.6 0.8 copy-start
  9.2 12.8 %copy-start.3 = (f32[64,128,128]{1,2,0:T(8,128)}, f32[64,128,128]{1,2,0:T(8,128)S(1)}, u32[]{:S(2)}) copy-start(f32[64,128,128]{1,2,0:T(8,128)S(1)} %bitcast_subtract_fusion) | copy-start | bytes 12582916
  12.9 2.5 %copy-start.5 = (f32[64,128,128]{2,1,0:T(8,128)S(1)}, f32[64,128,128]{2,1,0:T(8,128)}, u32[]{:S(2)}) copy-start(f32[64,128,128]{2,1,0:T(8,128)} %param.7) | copy-start | bytes 12582916
  12.9 2.5 %copy-start.21 = (f32[64,128]{1,0:T(8,128)S(1)}, f32[64,128]{1,0:T(8,128)}, u32[]{:S(2)}) copy-start(f32[64,128]{1,0:T(8,128)} %param.6) | copy-start | bytes 98308
  14.7 13.5 %copy-start.6 = (f32[8,128,128]{2,1,0:T(8,128)}, f32[8,128,128]{2,1,0:T(8,128)S(1)}, u32[]{:S(2)}) copy-start(f32[8,128,128]{2,1,0:T(8,128)S(1)} %fusion.42) | copy-start | bytes 1572868
  15.4 15.0 %copy-start.10 = (f32[1,2,128,128]{3,2,1,0:T(8,128)}, f32[1,2,128,128]{3,2,1,0:T(8,128)S(1)}, u32[]{:S(2)}) copy-start(f32[1,2,128,128]{3,2,1,0:T(8,128)S(1)} %convolution_bitcast_fusion.5) | copy-start | bytes 393220
  22.0 21.0 %copy-start.15 = (f32[64,1,128]{2,1,0:T(1,128)}, f32[64,1,128]{2,1,0:T(1,128)S(1)}, u32[]{:S(2)}) copy-start(f32[64,1,128]{2,1,0:T(1,128)S(1)} %fusion.148) | copy-start | bytes 98308
  30.2 0.6 copy-start.24
  42.3 0.8 copy-start.9
  47.2 0.6 copy-start.28
  48.1 0.7 copy-start.13
  63.7 18.2 %copy-start.4 = (f32[64,128,128]{1,2,0:T(8,128)S(1)}, f32[64,128,128]{1,2,0:T(8,128)}, u32[]{:S(2)}) copy-start(f32[64,128,128]{1,2,0:T(8,128)} %copy-done.3) | copy-start | bytes 12582916
  73.2 12.3 %copy-start.16 = (f32[64,1,128]{2,1,0:T(1,128)S(1)}, f32[64,1,128]{2,1,0:T(1,128)}, u32[]{:S(2)}) copy-start(f32[64,1,128]{2,1,0:T(1,128)} %copy-done.15) | copy-start | bytes 98308
  74.0 11.6 %copy-start.1 = (f32[64,128,128]{2,1,0:T(8,128)S(1)}, f32[64,128,128]{2,1,0:T(8,128)}, u32[]{:S(2)}) copy-start(f32[64,128,128]{2,1,0:T(8,128)} %param.8) | copy-start | bytes 12582916
  85.6 11.8 %copy-start.19 = (f32[64,128]{1,0:T(8,128)}, f32[64,128]{1,0:T(8,128)S(1)}, u32[]{:S(2)}) copy-start(f32[64,128]{1,0:T(8,128)S(1)} %add.160) | copy-start | bytes 98308
  87.8 2.7 %copy-start.14 = (f32[128,128]{1,0:T(8,128)S(1)}, f32[128,128]{1,0:T(8,128)}, u32[]{:S(2)}) copy-start(f32[128,128]{1,0:T(8,128)} %param.9) | copy-start | bytes 196612
  89.8 14.9 %copy-start.7 = (f32[8,128,128]{2,1,0:T(8,128)}, f32[8,128,128]{2,1,0:T(8,128)S(1)}, u32[]{:S(2)}) copy-start(f32[8,128,128]{2,1,0:T(8,128)S(1)} %fusion.45) | copy-start | bytes 1572868
  90.5 17.6 %copy-start.11 = (f32[1,2,128,128]{3,2,1,0:T(8,128)}, f32[1,2,128,128]{3,2,1,0:T(8,128)S(1)}, u32[]{:S(2)}) copy-start(f32[1,2,128,128]{3,2,1,0:T(8,128)S(1)} %convolution_bitcast_fusion.3) | copy-start | bytes 393220
  90.8 14.5 %copy-start.20 = (f32[64,128]{1,0:T(8,128)}, f32[64,128]{1,0:T(8,128)S(1)}, u32[]{:S(2)}) copy-start(f32[64,128]{1,0:T(8,128)S(1)} %fusion.150) | copy-start | bytes 98308
  97.4 7.8 %copy-start.17 = (f32[64,128]{1,0:T(8,128)}, f32[64,128]{1,0:T(8,128)S(1)}, u32[]{:S(2)}) copy-start(f32[64,128]{1,0:T(8,128)S(1)} %sub.13) | copy-start | bytes 98308
  106.8 0.6 copy-start.25
  121.2 19.9 %copy-start.12 = (f32[1,2,128,128]{3,2,1,0:T(8,128)S(1)}, f32[1,2,128,128]{3,2,1,0:T(8,128)}, u32[]{:S(2)}) copy-start(f32[1,2,128,128]{3,2,1,0:T(8,128)} %copy-done.11) | copy-start | bytes 393220
  121.2 20.0 %copy-start.26 = (f32[1,2,128]{2,1,0:T(2,128)S(1)}, f32[1,2,128]{2,1,0:T(2,128)}, u32[]{:S(2)}) copy-start(f32[1,2,128]{2,1,0:T(2,128)} %copy-done.25) | copy-start | bytes 3076
  121.2 20.5 %copy-start.29 = (f32[2,1,128]{2,1,0:T(1,128)S(1)}, f32[2,1,128]{2,1,0:T(1,128)}, u32[]{:S(2)}) copy-start(f32[2,1,128]{2,1,0:T(1,128)} %get-tuple-element.26) | copy-start | bytes 3076
  121.2 20.5 %copy-start.8 = (f32[8,128,128]{2,1,0:T(8,128)S(1)}, f32[8,128,128]{2,1,0:T(8,128)}, u32[]{:S(2)}) copy-start(f32[8,128,128]{2,1,0:T(8,128)} %copy-done.7) | copy-start | bytes 1572868
  121.3 20.9 %copy-start.27 = (f32[4,1,128]{2,1,0:T(1,128)S(1)}, f32[4,1,128]{2,1,0:T(1,128)}, u32[]{:S(2)}) copy-start(f32[4,1,128]{2,1,0:T(1,128)} %get-tuple-element.18) | copy-start | bytes 6148
  121.3 21.9 %copy-start.23 = (f32[8,1,128]{2,1,0:T(1,128)S(1)}, f32[8,1,128]{2,1,0:T(1,128)}, u32[]{:S(2)}) copy-start(f32[8,1,128]{2,1,0:T(1,128)} %get-tuple-element.14) | copy-start | bytes 12292
  122.2 22.7 %copy-start.22 = (f32[16,1,128]{2,1,0:T(1,128)S(1)}, f32[16,1,128]{2,1,0:T(1,128)}, u32[]{:S(2)}) copy-start(f32[16,1,128]{2,1,0:T(1,128)} %get-tuple-element.10) | copy-start | bytes 24580
  122.3 22.7 %copy-start.2 = (f32[64,128,128]{2,1,0:T(8,128)S(1)}, f32[64,128,128]{2,1,0:T(8,128)}, u32[]{:S(2)}) copy-start(f32[64,128,128]{2,1,0:T(8,128)} %param.8) | copy-start | bytes 12582916
  142.2 12.8 %copy-start.18 = (f32[64,128]{1,0:T(8,128)S(1)}, f32[64,128]{1,0:T(8,128)}, u32[]{:S(2)}) copy-start(f32[64,128]{1,0:T(8,128)} %copy-done.17) | copy-start | bytes 98308
where the time goes:
time: 159 us; the launch traced here: 156 us
  matrix products  84.7 us (53%)
  blocking collectives  51.2 us (32%)
  local copies, waits for them, and re-layouts  10.5 us (7%)
  other arithmetic  7.92 us (5%)
  between operations  1.61 us (1%)
    dot_general x42, matrix products, mv(): jnp.einsum('...ij,...j->...i', a, v, precision=exact, preferred_element_t...  61.1 us
    all_gather x2, blocking collectives, across(): gathered = lax.all_gather(pack(gm, gv), 'outer')  29.6 us
    all_gather x2, blocking collectives, group_level(): gathered = lax.all_gather(pack(mat, vec), axis)  21.6 us
    dot_general x23, matrix products, mm(): return jnp.matmul(a, b, precision=exact, preferred_element_type=jnp.float32)  17.7 us
    dot_general x1, matrix products, on_device(): jnp.einsum('tij,jk->tik', gains, mapped, precision=exact, preferred_eleme...  5.65 us
    slice x16, local copies, waits for them, and re-layouts, pair_up(): v1, v2 = (pv[..., first, :], pv[..., second, :])  4.94 us
    unnamed x61, local copies, waits for them, and re-layouts  4.69 us

commit v1 on v0

--- a/solution.py
+++ b/solution.py
@@ -12,7 +12,7 @@
 
 
 def mv(a, v):
-    return jnp.einsum("...ij,...j->...i", a, v, precision=exact, preferred_element_type=jnp.float32)
+    return jnp.sum(a * v[..., None, :], axis=-1)
 
 
 def pair_up(mats, vecs, backward):

time: 159 us -> 184 us (1.16)
  matrix products: 84.7 us -> 31.3 us
  local copies, waits for them, and re-layouts: 10.5 us -> 54.7 us
  other arithmetic: 7.92 us -> 41.5 us
    dot_general x42 -> x0, matrix products: 61.1 us -> none  [mv(): jnp.einsum('...ij,...j->...i', a, v, precision=exact, preferred_element_t...]
    reduce_sum x0 -> x40, other arithmetic: none -> 30.4 us  [mv(): return jnp.sum(a * v[..., None, :], axis=-1)]
    unnamed x61 -> x95, local copies, waits for them, and re-layouts: 4.69 us -> 31.9 us
    slice x0 -> x12, local copies, waits for them, and re-layouts: none -> 10.9 us  [the longest x11 9.45 us: pair_up(): m1, m2 = (pm[..., first, :, :], pm[..., second, :, :])]
    another operation x0 -> x4, local copies, waits for them, and re-layouts: none -> 8.19 us  [group_level(): both_m = jnp.stack((pm, mats), axis=0)]
    dot_general x23, matrix products: 17.7 us -> 25.6 us  [mm(): return jnp.matmul(a, b, precision=exact, preferred_element_type=jnp.float32)]
    slice x16 -> x10, local copies, waits for them, and re-layouts: 4.94 us -> 0.7 us  [pair_up(): v1, v2 = (pv[..., first, :], pv[..., second, :])]
    add x0 -> x15, other arithmetic: none -> 3.52 us  [the longest x6 1.38 us: spread(): other = mv(pm[:, 0], states) + pv[:, 0]]
where the time goes in v1:
time: 184 us; the launch traced here: 182 us
  local copies, waits for them, and re-layouts  54.7 us (30%)
  blocking collectives  52.5 us (29%)
  other arithmetic  41.5 us (23%)
  matrix products  31.3 us (17%)
  between operations  1.95 us (1%)
    unnamed x95, local copies, waits for them, and re-layouts  31.9 us
    reduce_sum x40, other arithmetic, mv(): return jnp.sum(a * v[..., None, :], axis=-1)  30.4 us
    all_gather x2, blocking collectives, across(): gathered = lax.all_gather(pack(gm, gv), 'outer')  29.7 us
    dot_general x23, matrix products, mm(): return jnp.matmul(a, b, precision=exact, preferred_element_type=jnp.float32)  25.6 us
    all_gather x2, blocking collectives, group_level(): gathered = lax.all_gather(pack(mat, vec), axis)  22.8 us
    slice x11, local copies, waits for them, and re-layouts, pair_up(): m1, m2 = (pm[..., first, :, :], pm[..., second, :, :])  9.45 us
    another operation x4, local copies, waits for them, and re-layouts, group_level(): both_m = jnp.stack((pm, mats), axis=0)  8.19 us
    dot_general x1, matrix products, on_device(): jnp.einsum('tij,jk->tik', gains, mapped, precision=exact, preferred_eleme...  5.47 us

profile of v1, /device:TPU:0, one launch (start us, length us, event | category | flops | bytes accessed | tf_op | source)
XLA Modules:
  0.0 182.0 jit_solution(1080736836586520092)
XLA Ops:
  0.7 3.4 %multiply_reduce_fusion.3 = f32[64,128]{1,0:T(8,128)S(1)} fusion(f32[64,128,128]{2,1,0:T(8,128)} %param.7, f32[64,128]{1,0:T(8,128)} %param.6), kind=kLoop, calls=%fused_computation.4 | loop fusion | flops 2088960 | bytes 4259840 | tf_op jit(solution)/shard_map/reduce_sum | solution.py:15
  5.1 5.5 %bitcast_subtract_fusion = f32[64,128,128]{1,2,0:T(8,128)S(1)} fusion(f32[128,128,1]{0,1,2:T(8,128)S(1)} %convolution_bitcast_fusion.6, f32[64,128,128]{2,1,0:T(8,128)} %param.7, f32[128,128]{0,1:T(8,128)S(1)} %copy.252), kind=kOutput, calls=%fused_computation | convolution fusion | flops 1611661312 | bytes 8519680 | tf_op jit(solution)/shard_map/tij,jk->tik/dot_general | solution.py:115
  10.6 1.9 %copy-done.3 = f32[64,128,128]{1,2,0:T(8,128)} copy-done((f32[64,128,128]{1,2,0:T(8,128)}, f32[64,128,128]{1,2,0:T(8,128)S(1)}, u32[]{:S(2)}) %copy-start.3) | copy-done | bytes 4194328
  12.5 1.5 slice.450
  14.0 1.9 %copy.325 = f32[32,1,128,128]{3,2,0,1:T(8,128)S(1)} copy(f32[32,1,128,128]{2,3,1,0:T(8,128)} %slice.450) | data formatting | bytes 4194304
  16.6 4.2 %fusion.2 = f32[32,128,128]{1,2,0:T(8,128)S(1)} fusion(f32[32,2,128,128]{2,3,1,0:T(8,128)} %bitcast.539), kind=kOutput, calls=%fused_computation.9 | convolution fusion | flops 805306368 | bytes 6291456 | tf_op jit(solution)/shard_map/dot_general | solution.py:11
  21.9 1.6 copy.327
  26.3 2.1 %copy.329 = f32[8,1,128,128]{3,2,0,1:T(8,128)} copy(f32[8,1,128,128]{2,3,1,0:T(8,128)} %slice.454) | data formatting | bytes 1048576
  33.1 1.4 fusion.35
  35.1 1.6 copy.333
  39.0 12.7 %all-gather.4 = f32[8,129,128]{2,1,0:T(8,128)} all-gather(f32[1,129,128]{2,1,0:T(8,128)S(1)} %maximum_bitcast_fusion), channel_id=2, replica_groups=mesh['outer'=4,'inner'=8] {'inner'}, dimensions={0}, use_global_device_ids=true | all-gather | bytes 594432 | tf_op jit(solution)/shard_map/all_gather | solution.py:88
  51.8 2.1 %broadcast_select_fusion.1 = (f32[8,128,128]{2,1,0:T(8,128)}, f32[8,128,128]{2,1,0:T(8,128)}) fusion(f32[128,128]{1,0:T(8,128)S(1)} %fusion.70, pred[8]{0:T(512)(128)(4,1)S(1)} %iota_compare_fusion.4, f32[8,129,128]{2,1,0:T(8,128)} %all-gather.4), kind=kLoop, calls=%fused_computation.91 | loop fusion | flops 131072 | bytes 1638408 | tf_op jit(solution)/shard_map/jit(_where)/select_n | solution.py:78
  53.9 2.1 %copy.266 = f32[1,4,2,128,128]{3,4,1,0,2:T(8,128)} copy(f32[1,4,2,128,128]{4,3,2,1,0:T(8,128)} %bitcast.571) | data formatting | bytes 1048576 | tf_op jit(solution)/shard_map/stack | solution.py:94
  55.9 2.0 %copy.267 = f32[1,4,2,128,128]{3,4,1,0,2:T(8,128)} copy(f32[1,4,2,128,128]{4,3,2,1,0:T(8,128)} %bitcast.569) | data formatting | bytes 1048576 | tf_op jit(solution)/shard_map/stack | solution.py:94
  58.0 1.8 fusion.22
  61.3 1.8 copy.335
  69.5 15.0 %all-gather.5 = f32[4,129,128]{2,1,0:T(8,128)} all-gather(f32[1,129,128]{2,1,0:T(8,128)S(1)} %maximum_bitcast_fusion.1), channel_id=3, replica_groups=mesh['outer'=4,'inner'=8] {'outer'}, dimensions={0}, use_global_device_ids=true | all-gather | bytes 330240 | tf_op jit(solution)/shard_map/all_gather | solution.py:102
  94.4 1.9 %multiply_reduce_fusion.5 = f32[32,128]{1,0:T(8,128)S(1)} fusion(f32[32,2,128,128]{2,3,1,0:T(8,128)} %bitcast.540, f32[32,128]{1,0:T(8,128)S(1)} %bitcast.586), kind=kLoop, calls=%fused_computation.16 | loop fusion | flops 1044480 | bytes 2129920 | tf_op jit(solution)/shard_map/reduce_sum | solution.py:15
  96.5 1.5 multiply_reduce_fusion.2
  100.6 3.5 %fusion = f32[32,128,128]{1,2,0:T(8,128)S(1)} fusion(f32[32,2,128,128]{3,2,1,0:T(8,128)S(1)} %bitcast.536), kind=kOutput, calls=%fused_computation.7 | convolution fusion | flops 805306368 | bytes 6291456 | tf_op jit(solution)/shard_map/dot_general | solution.py:11
  105.2 1.6 copy.342
  109.6 2.1 %copy.344 = f32[8,1,128,128]{3,2,0,1:T(8,128)} copy(f32[8,1,128,128]{2,3,1,0:T(8,128)} %slice.501) | data formatting | bytes 1048576
  121.4 1.6 copy.348
  129.5 10.1 %all-gather.6 = f32[8,129,128]{2,1,0:T(8,128)S(1)} all-gather(f32[1,129,128]{2,1,0:T(8,128)S(1)} %maximum_bitcast_fusion.2), channel_id=4, replica_groups=mesh['outer'=4,'inner'=8] {'inner'}, dimensions={0}, use_global_device_ids=true | all-gather | bytes 594432 | tf_op jit(solution)/shard_map/all_gather | solution.py:88
  141.5 2.0 %copy.298 = f32[1,4,2,128,128]{3,4,1,0,2:T(8,128)} copy(f32[1,4,2,128,128]{4,3,2,1,0:T(8,128)} %bitcast.572) | data formatting | bytes 1048576 | tf_op jit(solution)/shard_map/stack | solution.py:94
  143.5 2.0 %copy.299 = f32[1,4,2,128,128]{3,4,1,0,2:T(8,128)} copy(f32[1,4,2,128,128]{4,3,2,1,0:T(8,128)} %bitcast.570) | data formatting | bytes 1048576 | tf_op jit(solution)/shard_map/stack | solution.py:94
  145.6 1.8 fusion.18
  148.9 1.8 copy.349
  156.1 14.8 %all-gather.7 = f32[4,129,128]{2,1,0:T(8,128)S(1)} all-gather(f32[1,129,128]{2,1,0:T(8,128)S(1)} %maximum_bitcast_fusion.3), channel_id=5, replica_groups=mesh['outer'=4,'inner'=8] {'outer'}, dimensions={0}, use_global_device_ids=true | all-gather | bytes 330240 | tf_op jit(solution)/shard_map/all_gather | solution.py:102
  173.7 1.5 slice.496
  175.2 1.9 %copy.339 = f32[32,1,128,128]{2,3,0,1:T(8,128)S(1)} copy(f32[32,1,128,128]{3,2,1,0:T(8,128)} %slice.496) | data formatting | bytes 4194304
  178.0 3.3 %multiply_reduce_fusion = f32[64,128]{1,0:T(8,128)S(1)} fusion(f32[64,128,128]{2,1,0:T(8,128)} %param.8, f32[64,128]{1,0:T(8,128)S(1)} %bitcast.589), kind=kLoop, calls=%fused_computation.1 | loop fusion | flops 2088960 | bytes 4259840 | tf_op jit(solution)/shard_map/reduce_sum | solution.py:15
  (253 shorter events, 66.1 us)
Async XLA Ops:
  0.6 4.1 %copy-start = (f32[128,128]{1,0:T(8,128)S(1)}, f32[128,128]{1,0:T(8,128)}, u32[]{:S(2)}) copy-start(f32[128,128]{1,0:T(8,128)} %param.10) | copy-start | bytes 196612
  0.6 4.1 %copy-start.17 = (f32[128,128]{1,0:T(8,128)S(1)}, f32[128,128]{1,0:T(8,128)}, u32[]{:S(2)}) copy-start(f32[128,128]{1,0:T(8,128)} %param.9) | copy-start | bytes 196612
  10.6 1.9 %copy-start.3 = (f32[64,128,128]{1,2,0:T(8,128)}, f32[64,128,128]{1,2,0:T(8,128)S(1)}, u32[]{:S(2)}) copy-start(f32[64,128,128]{1,2,0:T(8,128)S(1)} %bitcast_subtract_fusion) | copy-start | bytes 12582916
  30.3 0.8 copy-start.7
  33.0 18.7 %copy-start.36 = (f32[2,2,128]{2,0,1:T(2,128)}, f32[2,2,128]{2,0,1:T(2,128)S(1)}, u32[]{:S(2)}) copy-start(f32[2,2,128]{2,0,1:T(2,128)S(1)} %copy_add_fusion.3) | copy-start | bytes 6148
  37.8 13.9 %copy-start.40 = (f32[1,2,128]{2,1,0:T(2,128)}, f32[1,2,128]{2,1,0:T(2,128)S(1)}, u32[]{:S(2)}) copy-start(f32[1,2,128]{2,1,0:T(2,128)S(1)} %fusion.87) | copy-start | bytes 3076
  59.8 0.8 copy-start.9
  68.9 0.7 copy-start.14
  84.5 9.2 %copy-start.33 = (f32[4,2,128]{2,1,0:T(2,128)S(1)}, f32[4,2,128]{2,1,0:T(2,128)}, u32[]{:S(2)}) copy-start(f32[4,2,128]{2,1,0:T(2,128)} %copy-done.32) | copy-start | bytes 12292
  84.5 9.5 %copy-start.29 = (f32[8,2,128]{2,1,0:T(2,128)S(1)}, f32[8,2,128]{2,1,0:T(2,128)}, u32[]{:S(2)}) copy-start(f32[8,2,128]{2,1,0:T(2,128)} %copy-done.28) | copy-start | bytes 24580
  91.8 4.6 %copy-start.16 = (f32[64,128]{1,0:T(8,128)S(1)}, f32[64,128]{1,0:T(8,128)}, u32[]{:S(2)}) copy-start(f32[64,128]{1,0:T(8,128)} %copy-done.15) | copy-start | bytes 98308
  92.5 4.0 %copy-start.4 = (f32[64,128,128]{1,2,0:T(8,128)S(1)}, f32[64,128,128]{1,2,0:T(8,128)}, u32[]{:S(2)}) copy-start(f32[64,128,128]{1,2,0:T(8,128)} %copy-done.3) | copy-start | bytes 12582916
  96.5 1.5 copy-start.18
  96.5 2.2 %copy-start.1 = (f32[64,128,128]{2,1,0:T(8,128)S(1)}, f32[64,128,128]{2,1,0:T(8,128)}, u32[]{:S(2)}) copy-start(f32[64,128,128]{2,1,0:T(8,128)} %param.8) | copy-start | bytes 12582916
  98.0 1.9 %copy-start.21 = (f32[64,128]{1,0:T(8,128)}, f32[64,128]{1,0:T(8,128)S(1)}, u32[]{:S(2)}) copy-start(f32[64,128]{1,0:T(8,128)S(1)} %add.275) | copy-start | bytes 98308
  98.7 1.2 copy-start.25
  99.9 4.2 %copy-start.19 = (f32[64,128]{1,0:T(8,128)}, f32[64,128]{1,0:T(8,128)S(1)}, u32[]{:S(2)}) copy-start(f32[64,128]{1,0:T(8,128)S(1)} %multiply_reduce_fusion.1) | copy-start | bytes 98308
  99.9 4.2 %copy-start.23 = (f32[8,8,128]{2,1,0:T(8,128)}, f32[8,8,128]{2,1,0:T(8,128)S(1)}, u32[]{:S(2)}) copy-start(f32[8,8,128]{2,1,0:T(8,128)S(1)} %add_subtract_fusion) | copy-start | bytes 98308
  112.9 1.2 copy-start.30
  114.1 0.8 copy-start.5
  139.7 0.8 copy-start.10
  147.4 0.8 copy-start.8
  151.6 21.0 %copy-start.12 = (f32[1,2,128,128]{2,3,1,0:T(8,128)S(1)}, f32[1,2,128,128]{2,3,1,0:T(8,128)}, u32[]{:S(2)}) copy-start(f32[1,2,128,128]{2,3,1,0:T(8,128)} %copy-done.11) | copy-start | bytes 393220
  151.6 21.1 %copy-start.38 = (f32[1,2,128]{2,1,0:T(2,128)S(1)}, f32[1,2,128]{2,1,0:T(2,128)}, u32[]{:S(2)}) copy-start(f32[1,2,128]{2,1,0:T(2,128)} %copy-done.37) | copy-start | bytes 3076
  152.9 19.9 %copy-start.35 = (f32[2,2,128]{2,0,1:T(2,128)S(1)}, f32[2,2,128]{2,0,1:T(2,128)}, u32[]{:S(2)}) copy-start(f32[2,2,128]{2,0,1:T(2,128)} %copy-done.34) | copy-start | bytes 6148
  152.9 20.0 %copy-start.6 = (f32[8,128,128]{1,2,0:T(8,128)S(1)}, f32[8,128,128]{1,2,0:T(8,128)}, u32[]{:S(2)}) copy-start(f32[8,128,128]{1,2,0:T(8,128)} %copy-done.5) | copy-start | bytes 1572868
  152.9 20.1 %copy-start.31 = (f32[4,2,128]{2,1,0:T(2,128)S(1)}, f32[4,2,128]{2,1,0:T(2,128)}, u32[]{:S(2)}) copy-start(f32[4,2,128]{2,1,0:T(2,128)} %copy-done.30) | copy-start | bytes 12292
  154.1 19.1 %copy-start.27 = (f32[8,2,128]{2,1,0:T(2,128)S(1)}, f32[8,2,128]{2,1,0:T(2,128)}, u32[]{:S(2)}) copy-start(f32[8,2,128]{2,1,0:T(2,128)} %copy-done.26) | copy-start | bytes 24580
  155.6 18.0 %copy-start.2 = (f32[64,128,128]{2,1,0:T(8,128)S(1)}, f32[64,128,128]{2,1,0:T(8,128)}, u32[]{:S(2)}) copy-start(f32[64,128,128]{2,1,0:T(8,128)} %param.8) | copy-start | bytes 12582916
  177.1 0.8 copy-start.24
  177.9 3.4 %copy-start.20 = (f32[64,128]{1,0:T(8,128)S(1)}, f32[64,128]{1,0:T(8,128)}, u32[]{:S(2)}) copy-start(f32[64,128]{1,0:T(8,128)} %copy-done.19) | copy-start | bytes 98308
  178.0 3.4 %copy-start.22 = (f32[64,128]{1,0:T(8,128)S(1)}, f32[64,128]{1,0:T(8,128)}, u32[]{:S(2)}) copy-start(f32[64,128]{1,0:T(8,128)} %copy-done.21) | copy-start | bytes 98308
  (9 other events, 5.5 us)
